TPU v7x, 256 devices: a whole 4x4x8 slice. The times are simulated.
256 devices in a mesh: blk: 64 (over z, x_lo, y), circ: 4 (over x_hi, core).
Axes of the slice: x: 4 (x_hi: 2, x_lo: 2; x = x_hi * 2 + x_lo), y: 4, z: 8, core: 2. Of those that a mesh axis runs over, the one named last changes fastest.
Arguments:
- panels: float32 [4, 8192], P(None, ('blk', 'circ')), may hold values from -2 to 2, as said below
- node_of_panel: int32 [8192], P(('blk', 'circ')), may hold values from 0 to 2047, as said below
- stiffener_rows: int32 [32], replicated, may hold values from 0 to 511
- density_start: float32 [16, 8192], P(None, ('blk', 'circ')), may hold values from -6 to 6
- motion_start: float32 [16, 512, 1024], P(None, 'blk', 'circ'), may hold values from -6 to 6
- force: float32 [16, 512, 1024], P(None, 'blk', 'circ'), may hold values from -128 to 128
- stiffness: float32 [512, 1024], P('blk', 'circ'), may hold values from 0.5 to 2
Outputs:
- source_density: float32 [16, 8192], P(None, ('blk', 'circ'))
- surface_pressure: float32 [16, 8192], P(None, ('blk', 'circ'))
- shell_motion: float32 [16, 512, 1024], P(None, 'blk', 'circ')
Inputs may be any that keep to these rules, and one draw needn't show every extreme that they name: `panels`: every panel lies between 0.98 and 1.02 from the z axis, with z between -2 and 2 and area between 0.5 and 2 times 8 pi / 8192. `node_of_panel`: counted as row * 256 + column within the tile of the device that holds the panel. `stiffener_rows`: A row may be listed more than once.
All inputs are finite; a program needn't handle non-finite values.
Results may differ from a plain program's by a relative error of at most 0.0029.
Values may be sent and summed in bfloat16 or wider, within the bound.
No kernel may reach another device: no remote copies, remote signals or barrier semaphores. Data moves between devices by JAX's collectives and lax.ppermute only.
A program may use at most 64 MiB of HBM per device.

v0:
```python
import math
import jax
import jax.numpy as jnp
from jax import lax
from jax.sharding import PartitionSpec as P

ITERS = 4
SWEEPS = 2
wave_number = 4.0
single_scale = 30.0
double_scale = 6.0
hoop_spring = 40.0
inertia_term = 4.0
loss_factor = 0.2
relaxation = 0.3


def padded(block, sides, width):
    for axis, dim in sides:
        count = lax.axis_size(axis)
        forward = [(i, i + 1) for i in range(count - 1)]
        forward.append((count - 1, 0))
        backward = [(target, source) for source, target in forward]
        low = lax.ppermute(
            lax.slice_in_dim(block, block.shape[dim] - width, None, axis=dim), axis, forward
        )
        high = lax.ppermute(lax.slice_in_dim(block, 0, width, axis=dim), axis, backward)
        block = jnp.concatenate([low, block, high], axis=dim)
    return block


def kernel_blocks(targets, sources):
    radial = jnp.sqrt(targets[0] * targets[0] + targets[1] * targets[1])
    normal_x = (targets[0] / radial)[:, None]
    normal_y = (targets[1] / radial)[:, None]
    delta_x = targets[0][:, None] - sources[0][None, :]
    delta_y = targets[1][:, None] - sources[1][None, :]
    delta_z = targets[2][:, None] - sources[2][None, :]
    areas = sources[3][None, :]
    dist_sq = delta_x * delta_x + delta_y * delta_y + delta_z * delta_z + areas / math.pi
    distance = jnp.sqrt(dist_sq)
    inverse = 1.0 / distance
    phase_arg = wave_number * distance
    cosine = jnp.cos(phase_arg)
    sine_part = jnp.sin(phase_arg)
    weight = areas * (1.0 / (4.0 * math.pi)) * inverse
    single = single_scale * weight
    double = double_scale * weight * (normal_x * delta_x + normal_y * delta_y) * inverse * inverse
    real_stack = jnp.concatenate(
        [single * cosine, double * (-cosine - phase_arg * sine_part)], axis=0
    )
    imag_stack = jnp.concatenate(
        [single * sine_part, double * (phase_arg * cosine - sine_part)], axis=0
    )
    return (real_stack.astype(jnp.bfloat16), imag_stack.astype(jnp.bfloat16))


def form_kernels(targets, sources):
    width = sources.shape[1]
    block_cols = math.gcd(width, 1024)
    block_count = width // block_cols
    source_blocks = jnp.transpose(sources.reshape(4, block_count, block_cols), (1, 0, 2))
    real_blocks, imag_blocks = lax.map(lambda block: kernel_blocks(targets, block), source_blocks)
    rows_out = real_blocks.shape[1]
    real_stack = jnp.transpose(real_blocks, (1, 0, 2)).reshape(rows_out, width)
    imag_stack = jnp.transpose(imag_blocks, (1, 0, 2)).reshape(rows_out, width)
    return (real_stack, imag_stack)


def fold_columns(real_stack, imag_stack):

    def fold_step(running, shard_piece, first_col):
        half = shard_piece.shape[0] // 2
        rotated = jnp.concatenate([-shard_piece[half:], shard_piece[:half]], axis=0)
        first = jnp.einsum("lc,rc->lr", shard_piece, real_stack, preferred_element_type=jnp.float32)
        second = jnp.einsum("lc,rc->lr", rotated, imag_stack, preferred_element_type=jnp.float32)
        return first + second

    return fold_step


def laplace_inner(extended):
    return (
        extended[..., 2:, 1:-1]
        + extended[..., :-2, 1:-1]
        + extended[..., 1:-1, 2:]
        + extended[..., 1:-1, :-2]
        - 4.0 * extended[..., 1:-1, 1:-1]
    )


def clear_outside(extended, width, blk_index, axial):
    total_rows = axial * lax.axis_size("blk")
    rows_here = blk_index * axial - width + jnp.arange(axial + 2 * width, dtype=jnp.int32)
    inside = (rows_here >= 0) & (rows_here < total_rows)
    return jnp.where(inside[:, None], extended, 0.0)


def relax(motion, bend, load, stiffness, hoop_rows):
    half = motion.shape[0] // 2
    shift = hoop_spring * hoop_rows - inertia_term
    applied_re = bend[:half] - loss_factor * bend[half:] + shift * motion[:half]
    applied_im = bend[half:] + loss_factor * bend[:half] + shift * motion[half:]
    resid_re = load[:half] - applied_re
    resid_im = load[half:] - applied_im
    diag_re = 20.0 * stiffness + shift
    diag_im = 20.0 * loss_factor * stiffness
    denom = diag_re * diag_re + diag_im * diag_im
    update_re = (resid_re * diag_re + resid_im * diag_im) / denom
    update_im = (resid_im * diag_re - resid_re * diag_im) / denom
    return motion + relaxation * jnp.concatenate([update_re, update_im], axis=0)


def per_device(
    panels, node_of_panel, stiffener_rows, density_start, motion_start, force, stiffness
):
    panel_dev = panels.shape[1]
    channels = density_start.shape[0]
    axial, circum = stiffness.shape
    blk_index = lax.axis_index("blk")
    devices = lax.axis_size("blk") * lax.axis_size("circ")
    rows_global = blk_index * axial + jnp.arange(axial, dtype=jnp.int32)
    hoop_rows = jnp.any(rows_global[:, None] == stiffener_rows[None, :], axis=1).astype(
        jnp.float32
    )[:, None]
    panel_weight = panels[3] * (panel_dev * devices / (8.0 * math.pi))
    sources = lax.all_gather(panels, ("blk", "circ"), axis=1, tiled=True)
    target_rows = panels.shape[1]
    real_stack, imag_stack = form_kernels(panels, sources)
    fold_step = fold_columns(real_stack, imag_stack)
    density = density_start
    motion = motion_start
    pressure = jnp.zeros_like(density_start)
    for round_index in range(ITERS):
        flat_motion = motion.reshape(channels, axial * circum)
        neumann = jnp.take(flat_motion, node_of_panel, axis=1)
        density_bf = density.astype(jnp.bfloat16)
        start_sum = jnp.zeros((channels, 2 * target_rows), jnp.float32)
        combined = fold_step(
            start_sum, lax.all_gather(density_bf, ("blk", "circ"), axis=1, tiled=True), jnp.int32(0)
        )
        single_part = combined[:, :target_rows]
        double_part = combined[:, target_rows:]
        pressure = single_part
        density = 0.5 * density + neumann - double_part
        fluid = jnp.zeros((channels, axial * circum), jnp.float32)
        fluid = fluid.at[:, node_of_panel].add(panel_weight[None, :] * pressure)
        load = force - fluid.reshape(channels, axial, circum)
        for sweep_index in range(SWEEPS):
            motion_ext = padded(motion, (("blk", 1), ("circ", 2)), 1)
            motion_ext = clear_outside(motion_ext, 1, blk_index, axial)
            moment = stiffness * laplace_inner(motion_ext)
            moment_ext = padded(moment, (("blk", 1), ("circ", 2)), 1)
            moment_ext = clear_outside(moment_ext, 1, blk_index, axial)
            bend = laplace_inner(moment_ext)
            motion = relax(motion, bend, load, stiffness, hoop_rows)
    return (density, pressure, motion)


def solution(mesh):
    in_specs = (
        P(None, ("blk", "circ")),
        P(("blk", "circ")),
        P(),
        P(None, ("blk", "circ")),
        P(None, "blk", "circ"),
        P(None, "blk", "circ"),
        P("blk", "circ"),
    )
    out_specs = (P(None, ("blk", "circ")), P(None, ("blk", "circ")), P(None, "blk", "circ"))
    return jax.shard_map(
        per_device, mesh=mesh, in_specs=in_specs, out_specs=out_specs, check_vma=False
    )
```

profile of v0, /device:TPU:1, one launch (start us, length us, event | category | flops | bytes accessed | tf_op | source)
XLA Modules:
  0.0 2012.5 jit_solution(11817012427763911444)
XLA Ops:
  1.6 9.8 collective-permute-start.1
  13.5 347.8 %all-gather = f32[256,32,4]{1,2,0:T(4,128)S(1)} all-gather(f32[1,32,4]{1,2,0:T(4,128)S(1)} %bitcast.201), channel_id=1, replica_groups=mesh['blk'=64,'circ'=4] {'blk','circ'}, dimensions={0}, use_global_device_ids=true | all-gather | bytes 131584 | tf_op jit(solution)/shard_map/all_gather | solution.py:127
  361.7 11.7 while.15
  375.7 341.9 %all-gather.1 = bf16[256,32,16]{1,2,0:T(8,128)(2,1)S(1)} all-gather(bf16[1,32,16]{1,2,0:T(8,128)(2,1)S(1)} %convert_bitcast_fusion.3), channel_id=1, replica_groups=mesh['blk'=64,'circ'=4] {'blk','circ'}, dimensions={0}, use_global_device_ids=true | all-gather | bytes 263168 | tf_op jit(solution)/shard_map/all_gather | solution.py:140
  723.7 344.9 %all-gather.2 = bf16[256,32,16]{1,2,0:T(8,128)(2,1)S(1)} all-gather(bf16[1,32,16]{1,2,0:T(8,128)(2,1)S(1)} %get-tuple-element.276), channel_id=1, replica_groups=mesh['blk'=64,'circ'=4] {'blk','circ'}, dimensions={0}, use_global_device_ids=true | all-gather | bytes 263168 | tf_op jit(solution)/shard_map/all_gather | solution.py:140
  1074.5 1.6 fusion.145
  1076.8 3.1 collective-permute-start.2
  1079.9 4.0 collective-permute-done.3
  1087.1 4.3 collective-permute-done.4
  1091.6 1.6 collective-permute-start.7
  1093.2 1.7 collective-permute-start.6
  1095.0 3.3 collective-permute-done.7
  1099.3 1.7 collective-permute-start.8
  1101.7 4.8 collective-permute-done.8
  1106.6 2.6 collective-permute-start.11
  1109.2 1.9 collective-permute-start.10
  1111.0 3.4 collective-permute-done.11
  1117.6 4.3 collective-permute-done.12
  1122.1 2.5 collective-permute-start.15
  1125.9 2.6 collective-permute-done.15
  1131.9 4.3 collective-permute-done.16
  1136.4 3.3 collective-permute-start.19
  1139.7 2.0 collective-permute-start.18
  1141.7 3.5 collective-permute-done.19
  1149.2 4.0 collective-permute-done.20
  1153.4 2.5 collective-permute-start.23
  1157.4 2.9 collective-permute-done.23
  1163.2 349.0 %all-gather.3 = bf16[256,32,16]{1,2,0:T(8,128)(2,1)S(1)} all-gather(bf16[1,32,16]{1,2,0:T(8,128)(2,1)S(1)} %get-tuple-element.171), channel_id=1, replica_groups=mesh['blk'=64,'circ'=4] {'blk','circ'}, dimensions={0}, use_global_device_ids=true | all-gather | bytes 263168 | tf_op jit(solution)/shard_map/all_gather | solution.py:140
  1512.5 1.9 reshape.1240
  1514.8 3.1 collective-permute-start.26
  1517.9 3.6 collective-permute-done.27
  1524.7 4.3 collective-permute-done.28
  1530.7 2.5 collective-permute-start.30
  1533.6 2.4 collective-permute-done.31
  1539.3 344.8 %all-gather.4 = bf16[256,32,16]{1,2,0:T(8,128)(2,1)S(1)} all-gather(bf16[1,32,16]{1,2,0:T(8,128)(2,1)S(1)} %get-tuple-element.274), channel_id=1, replica_groups=mesh['blk'=64,'circ'=4] {'blk','circ'}, dimensions={0}, use_global_device_ids=true | all-gather | bytes 263168 | tf_op jit(solution)/shard_map/all_gather | solution.py:140
  1884.4 1.9 reshape.1242
  1890.0 4.3 collective-permute-done.32
  1895.8 2.6 collective-permute-start.34
  1898.8 2.2 collective-permute-done.35
  1906.7 1.8 collective-permute-done.36
  1908.7 3.6 collective-permute-start.39
  1912.2 2.0 collective-permute-start.38
  1914.3 3.5 collective-permute-done.39
  1921.2 4.5 collective-permute-done.40
  1925.9 3.3 collective-permute-start.43
  1929.2 2.2 collective-permute-start.42
  1931.4 3.8 collective-permute-done.43
  1938.4 4.3 collective-permute-done.44
  1942.9 2.1 collective-permute-start.47
  1946.3 2.6 collective-permute-done.47
  1952.3 4.7 collective-permute-done.48
  1957.1 3.0 collective-permute-start.51
  1960.1 2.2 collective-permute-start.50
  1962.3 3.0 collective-permute-done.51
  1968.6 4.3 collective-permute-done.52
  1973.0 2.6 collective-permute-start.55
  1977.2 3.1 collective-permute-done.55
  1983.7 4.3 collective-permute-done.56
  1988.1 2.8 collective-permute-start.59
  1990.9 1.8 collective-permute-start.58
  1992.7 3.3 collective-permute-done.59
  1999.3 4.3 collective-permute-done.60
  2003.8 2.5 collective-permute-start.63
  2008.5 2.4 collective-permute-done.63
  (323 shorter events, 99.0 us)
Async XLA Ops:
  1.6 1074.7 %collective-permute-start.1 = (f32[16,1,256]{2,1,0:T(1,128)S(1)}, f32[16,1,256]{2,1,0:T(1,128)S(1)}, u32[]{:S(2)}, u32[]{:S(2)}) collective-permute-start(f32[16,1,256]{2,1,0:T(1,128)S(1)} %get-tuple-element.272), channel_id=1, source_target_pairs={{4,0},{8,4},{12,8},{16,12},{20,16},{24,20},{28,24},{32,28},{36,32}... | collective-permute-start | bytes 49160 | tf_op jit(solution)/shard_map/ppermute | solution.py:27
  11.5 1064.9 %collective-permute-start = (f32[16,1,256]{2,1,0:T(1,128)S(1)}, f32[16,1,256]{2,1,0:T(1,128)S(1)}, u32[]{:S(2)}, u32[]{:S(2)}) collective-permute-start(f32[16,1,256]{2,1,0:T(1,128)S(1)} %get-tuple-element.271), channel_id=1, source_target_pairs={{0,4},{4,8},{8,12},{12,16},{16,20},{20,24},{24,28},{28,32},{32,36}... | collective-permute-start | bytes 49160 | tf_op jit(solution)/shard_map/ppermute | solution.py:24
  1076.5 7.3 collective-permute-start.3
  1076.8 7.1 collective-permute-start.2
  1084.4 2.7 collective-permute-start.5
  1084.5 6.9 collective-permute-start.4
  1091.6 6.7 collective-permute-start.7
  1093.2 5.1 collective-permute-start.6
  1099.0 2.7 collective-permute-start.9
  1099.3 7.2 collective-permute-start.8
  1106.6 7.8 collective-permute-start.11
  1109.2 5.2 collective-permute-start.10
  1115.0 2.7 collective-permute-start.13
  1115.1 6.9 collective-permute-start.12
  1122.1 6.4 collective-permute-start.15
  1124.6 3.9 collective-permute-start.14
  1129.2 2.7 collective-permute-start.17
  1129.3 6.9 collective-permute-start.16
  1136.4 8.9 collective-permute-start.19
  1139.7 5.6 collective-permute-start.18
  1146.4 2.8 collective-permute-start.21
  1146.4 6.8 collective-permute-start.20
  1153.4 6.9 collective-permute-start.23
  1155.9 4.4 collective-permute-start.22
  1161.7 352.7 %collective-permute-start.25 = (f32[16,1,256]{2,1,0:T(1,128)S(1)}, f32[16,1,256]{2,1,0:T(1,128)S(1)}, u32[]{:S(2)}, u32[]{:S(2)}) collective-permute-start(f32[16,1,256]{2,1,0:T(1,128)S(1)} %get-tuple-element.258), channel_id=1, source_target_pairs={{4,0},{8,4},{12,8},{16,12},{20,16},{24,20},{28,24},{32,28},{36,32}... | collective-permute-start | bytes 49160 | tf_op jit(solution)/shard_map/ppermute | solution.py:27
  1161.7 352.7 %collective-permute-start.24 = (f32[16,1,256]{2,1,0:T(1,128)S(1)}, f32[16,1,256]{2,1,0:T(1,128)S(1)}, u32[]{:S(2)}, u32[]{:S(2)}) collective-permute-start(f32[16,1,256]{2,1,0:T(1,128)S(1)} %get-tuple-element.257), channel_id=1, source_target_pairs={{0,4},{4,8},{8,12},{12,16},{16,20},{20,24},{24,28},{28,32},{32,36}... | collective-permute-start | bytes 49160 | tf_op jit(solution)/shard_map/ppermute | solution.py:24
  1514.6 6.9 collective-permute-start.27
  1514.8 6.7 collective-permute-start.26
  1522.1 2.7 collective-permute-start.29
  1522.2 6.9 collective-permute-start.28
  1529.2 6.8 collective-permute-start.31
  1530.7 5.3 collective-permute-start.30
  1887.3 2.7 collective-permute-start.33
  1887.4 6.9 collective-permute-start.32
  1894.4 6.5 collective-permute-start.35
  1895.8 5.1 collective-permute-start.34
  1901.5 5.1 collective-permute-start.37
  1901.6 6.9 collective-permute-start.36
  1908.7 9.2 collective-permute-start.39
  1912.2 5.6 collective-permute-start.38
  1918.5 2.7 collective-permute-start.41
  1918.9 6.8 collective-permute-start.40
  1925.9 9.3 collective-permute-start.43
  1929.2 6.0 collective-permute-start.42
  1935.8 2.7 collective-permute-start.45
  1935.9 6.9 collective-permute-start.44
  1942.9 6.0 collective-permute-start.47
  1945.0 3.9 collective-permute-start.46
  1949.6 2.7 collective-permute-start.49
  1950.1 6.8 collective-permute-start.48
  1957.1 8.2 collective-permute-start.51
  1960.1 5.2 collective-permute-start.50
  1965.9 2.7 collective-permute-start.53
  1966.0 6.9 collective-permute-start.52
  1973.0 7.2 collective-permute-start.55
  1975.7 4.6 collective-permute-start.54
  1981.0 2.7 collective-permute-start.57
  1981.1 6.9 collective-permute-start.56
  1988.1 8.0 collective-permute-start.59
  1990.9 5.1 collective-permute-start.58
  1996.6 2.7 collective-permute-start.61
  1996.7 6.9 collective-permute-start.60
  2003.8 7.2 collective-permute-start.63
  2006.3 4.6 collective-permute-start.62
  (19 other events, 2934.6 us)
where the time goes:
time: 2020 us; the launch traced here: 2010 us
  blocking collectives  1730 us (86%)
  waiting for transfers between devices  120 us (6%)
  starting transfers between devices  101 us (5%)
  other arithmetic  31.7 us (2%)
  local copies, waits for them, and re-layouts  24.9 us (1%)
    all_gather x4, blocking collectives, per_device(): lax.all_gather(density_bf, ('blk', 'circ'), axis=1, tiled=True)  1380 us
    all_gather x1, blocking collectives, per_device(): sources = lax.all_gather(panels, ('blk', 'circ'), axis=1, tiled=True)  348 us
    ppermute x32, waiting for transfers between devices, padded(): lax.ppermute(lax.slice_in_dim(block, 0, width, axis=dim), axis, backward)  61.1 us
    ppermute x32, waiting for transfers between devices, padded(): lax.ppermute(lax.slice_in_dim(block, block.shape[dim] - width, None, axis...  58.7 us
    ppermute x32, starting transfers between devices, padded(): lax.ppermute(lax.slice_in_dim(block, block.shape[dim] - width, None, axis...  53.5 us
    ppermute x32, starting transfers between devices, padded(): lax.ppermute(lax.slice_in_dim(block, 0, width, axis=dim), axis, backward)  47.8 us
  transfers between devices with their start and end apart: 64, of which 42 were waited for; matrix products, arithmetic and copies ran while one was open for 2% of the time, Pallas kernels for 0%

commit v1 on v0

--- a/solution.py
+++ b/solution.py
@@ -114,6 +114,12 @@
 def per_device(
     panels, node_of_panel, stiffener_rows, density_start, motion_start, force, stiffness
 ):
+
+    def return_all_panel(mat, row_axis):
+        row_out = jnp.stack([mat for _ in range(jax.lax.axis_size(row_axis))])
+        then = jax.lax.all_to_all(row_out, row_axis, 0, 0)
+        return jnp.concatenate(then, axis=1)
+
     panel_dev = panels.shape[1]
     channels = density_start.shape[0]
     axial, circum = stiffness.shape
@@ -124,7 +130,7 @@
         jnp.float32
     )[:, None]
     panel_weight = panels[3] * (panel_dev * devices / (8.0 * math.pi))
-    sources = lax.all_gather(panels, ("blk", "circ"), axis=1, tiled=True)
+    sources = return_all_panel(panels, ("blk", "circ"))
     target_rows = panels.shape[1]
     real_stack, imag_stack = form_kernels(panels, sources)
     fold_step = fold_columns(real_stack, imag_stack)

time: 2020 us -> 1700 us (0.84)
  blocking collectives: 1730 us -> 1390 us
    all_gather x1 -> x0, blocking collectives: 348 us -> none  [per_device(): sources = lax.all_gather(panels, ('blk', 'circ'), axis=1, tiled=True)]
  transfers between devices with their start and end apart: 64 -> 65, of which waited for: 42 -> 42; matrix products, arithmetic and copies ran while one was open for 2% -> 1% of each run, Pallas kernels for 0% -> 0%
where the time goes in v1:
time: 1700 us; the launch traced here: 1690 us
  blocking collectives  1390 us (82%)
  waiting for transfers between devices  118 us (7%)
  starting transfers between devices  116 us (7%)
  other arithmetic  33.1 us (2%)
  local copies, waits for them, and re-layouts  25.8 us (2%)
    all_gather x4, blocking collectives, per_device(): lax.all_gather(density_bf, ('blk', 'circ'), axis=1, tiled=True)  1390 us
    ppermute x32, waiting for transfers between devices, padded(): lax.ppermute(lax.slice_in_dim(block, 0, width, axis=dim), axis, backward)  60.2 us
    ppermute x32, waiting for transfers between devices, padded(): lax.ppermute(lax.slice_in_dim(block, block.shape[dim] - width, None, axis...  57.7 us
    ppermute x32, starting transfers between devices, padded(): lax.ppermute(lax.slice_in_dim(block, block.shape[dim] - width, None, axis...  55.7 us
    ppermute x32, starting transfers between devices, padded(): lax.ppermute(lax.slice_in_dim(block, 0, width, axis=dim), axis, backward)  45 us
  transfers between devices with their start and end apart: 65, of which 42 were waited for; matrix products, arithmetic and copies ran while one was open for 1% of the time, Pallas kernels for 0%

profile of v1, /device:TPU:1, one launch (start us, length us, event | category | flops | bytes accessed | tf_op | source)
XLA Modules:
  0.0 1686.1 jit_solution(4721546688162398791)
XLA Ops:
  2.4 15.6 all-to-all-start
  18.1 7.6 collective-permute-start.1
  25.8 349.6 %all-gather = bf16[256,32,16]{1,2,0:T(8,128)(2,1)S(1)} all-gather(bf16[1,32,16]{1,2,0:T(8,128)(2,1)S(1)} %convert_bitcast_fusion.3), channel_id=1, replica_groups=mesh['blk'=64,'circ'=4] {'blk','circ'}, dimensions={0}, use_global_device_ids=true | all-gather | bytes 263168 | tf_op jit(solution)/shard_map/all_gather | solution.py:146
  379.4 3.1 collective-permute-start.2
  382.5 3.6 collective-permute-done.3
  389.4 4.3 collective-permute-done.4
  395.3 2.3 collective-permute-start.6
  398.8 2.0 collective-permute-done.7
  404.1 11.7 while.15
  418.5 344.4 %all-gather.1 = bf16[256,32,16]{1,2,0:T(8,128)(2,1)S(1)} all-gather(bf16[1,32,16]{1,2,0:T(8,128)(2,1)S(1)} %get-tuple-element.276), channel_id=1, replica_groups=mesh['blk'=64,'circ'=4] {'blk','circ'}, dimensions={0}, use_global_device_ids=true | all-gather | bytes 263168 | tf_op jit(solution)/shard_map/all_gather | solution.py:146
  763.1 1.9 reshape.1238
  770.9 1.7 fusion.145
  775.4 4.3 collective-permute-done.8
  781.3 3.0 collective-permute-start.10
  784.3 2.3 collective-permute-done.11
  789.8 4.3 collective-permute-done.12
  794.3 3.6 collective-permute-start.15
  797.9 1.7 collective-permute-start.14
  799.6 3.2 collective-permute-done.15
  806.1 4.3 collective-permute-done.16
  810.6 2.7 collective-permute-start.19
  813.3 1.7 collective-permute-start.18
  815.0 3.2 collective-permute-done.19
  822.1 4.0 collective-permute-done.20
  826.3 2.7 collective-permute-start.23
  829.0 1.8 collective-permute-start.22
  830.8 3.2 collective-permute-done.23
  837.4 348.3 %all-gather.2 = bf16[256,32,16]{1,2,0:T(8,128)(2,1)S(1)} all-gather(bf16[1,32,16]{1,2,0:T(8,128)(2,1)S(1)} %get-tuple-element.171), channel_id=1, replica_groups=mesh['blk'=64,'circ'=4] {'blk','circ'}, dimensions={0}, use_global_device_ids=true | all-gather | bytes 263168 | tf_op jit(solution)/shard_map/all_gather | solution.py:146
  1186.0 1.9 reshape.1240
  1188.3 3.1 collective-permute-start.26
  1191.4 3.6 collective-permute-done.27
  1198.2 4.3 collective-permute-done.28
  1204.1 2.1 collective-permute-start.30
  1206.6 3.3 collective-permute-done.31
  1213.2 344.2 %all-gather.3 = bf16[256,32,16]{1,2,0:T(8,128)(2,1)S(1)} all-gather(bf16[1,32,16]{1,2,0:T(8,128)(2,1)S(1)} %get-tuple-element.274), channel_id=1, replica_groups=mesh['blk'=64,'circ'=4] {'blk','circ'}, dimensions={0}, use_global_device_ids=true | all-gather | bytes 263168 | tf_op jit(solution)/shard_map/all_gather | solution.py:146
  1557.6 1.9 reshape.1242
  1563.2 4.3 collective-permute-done.32
  1569.1 3.0 collective-permute-start.34
  1572.4 2.2 collective-permute-done.35
  1580.3 1.8 collective-permute-done.36
  1582.3 3.4 collective-permute-start.39
  1585.7 2.3 collective-permute-start.38
  1588.0 3.1 collective-permute-done.39
  1594.5 4.4 collective-permute-done.40
  1599.1 3.8 collective-permute-start.43
  1602.9 2.1 collective-permute-start.42
  1604.9 3.6 collective-permute-done.43
  1611.8 4.3 collective-permute-done.44
  1616.3 2.3 collective-permute-start.47
  1619.9 2.9 collective-permute-done.47
  1626.1 4.3 collective-permute-done.48
  1630.6 3.0 collective-permute-start.51
  1633.6 2.0 collective-permute-start.50
  1635.6 3.5 collective-permute-done.51
  1642.6 4.3 collective-permute-done.52
  1647.1 2.4 collective-permute-start.55
  1650.8 2.9 collective-permute-done.55
  1657.0 4.3 collective-permute-done.56
  1661.5 3.0 collective-permute-start.59
  1664.5 2.0 collective-permute-start.58
  1666.5 3.5 collective-permute-done.59
  1673.3 4.3 collective-permute-done.60
  1677.8 2.4 collective-permute-start.63
  1682.1 2.2 collective-permute-done.63
  (334 shorter events, 101.4 us)
Async XLA Ops:
  2.4 399.7 %all-to-all-start = ((f32[256,1,128]{2,1,0:T(1,128)}), f32[256,1,128]{2,1,0:T(1,128)S(1)}, u32[]{:S(2)}, u32[]{:S(2)}) async-start(f32[256,1,128]{2,1,0:T(1,128)} %reshape.1259), calls=%async_computation | async-start | bytes 262144 | tf_op jit(solution)/shard_map/all_to_all | solution.py:120
  18.1 360.9 %collective-permute-start.1 = (f32[16,1,256]{2,1,0:T(1,128)S(1)}, f32[16,1,256]{2,1,0:T(1,128)S(1)}, u32[]{:S(2)}, u32[]{:S(2)}) collective-permute-start(f32[16,1,256]{2,1,0:T(1,128)S(1)} %get-tuple-element.272), channel_id=1, source_target_pairs={{4,0},{8,4},{12,8},{16,12},{20,16},{24,20},{28,24},{32,28},{36,32}... | collective-permute-start | bytes 49160 | tf_op jit(solution)/shard_map/ppermute | solution.py:27
  25.7 353.3 %collective-permute-start = (f32[16,1,256]{2,1,0:T(1,128)S(1)}, f32[16,1,256]{2,1,0:T(1,128)S(1)}, u32[]{:S(2)}, u32[]{:S(2)}) collective-permute-start(f32[16,1,256]{2,1,0:T(1,128)S(1)} %get-tuple-element.271), channel_id=1, source_target_pairs={{0,4},{4,8},{8,12},{12,16},{16,20},{20,24},{24,28},{28,32},{32,36}... | collective-permute-start | bytes 49160 | tf_op jit(solution)/shard_map/ppermute | solution.py:24
  379.2 6.9 collective-permute-start.3
  379.4 6.7 collective-permute-start.2
  386.7 2.7 collective-permute-start.5
  386.8 6.9 collective-permute-start.4
  393.8 7.1 collective-permute-start.7
  395.3 5.6 collective-permute-start.6
  772.7 2.7 collective-permute-start.9
  772.8 6.9 collective-permute-start.8
  779.9 6.8 collective-permute-start.11
  781.3 5.4 collective-permute-start.10
  787.2 2.7 collective-permute-start.13
  787.3 6.9 collective-permute-start.12
  794.3 8.4 collective-permute-start.15
  797.9 4.9 collective-permute-start.14
  803.5 2.7 collective-permute-start.17
  803.6 6.9 collective-permute-start.16
  810.6 7.6 collective-permute-start.19
  813.3 4.9 collective-permute-start.18
  819.3 2.8 collective-permute-start.21
  819.3 6.8 collective-permute-start.20
  826.3 7.7 collective-permute-start.23
  829.0 5.1 collective-permute-start.22
  835.4 352.4 %collective-permute-start.25 = (f32[16,1,256]{2,1,0:T(1,128)S(1)}, f32[16,1,256]{2,1,0:T(1,128)S(1)}, u32[]{:S(2)}, u32[]{:S(2)}) collective-permute-start(f32[16,1,256]{2,1,0:T(1,128)S(1)} %get-tuple-element.258), channel_id=1, source_target_pairs={{4,0},{8,4},{12,8},{16,12},{20,16},{24,20},{28,24},{32,28},{36,32}... | collective-permute-start | bytes 49160 | tf_op jit(solution)/shard_map/ppermute | solution.py:27
  835.9 351.9 %collective-permute-start.24 = (f32[16,1,256]{2,1,0:T(1,128)S(1)}, f32[16,1,256]{2,1,0:T(1,128)S(1)}, u32[]{:S(2)}, u32[]{:S(2)}) collective-permute-start(f32[16,1,256]{2,1,0:T(1,128)S(1)} %get-tuple-element.257), channel_id=1, source_target_pairs={{0,4},{4,8},{8,12},{12,16},{16,20},{20,24},{24,28},{28,32},{32,36}... | collective-permute-start | bytes 49160 | tf_op jit(solution)/shard_map/ppermute | solution.py:24
  1188.0 6.9 collective-permute-start.27
  1188.3 6.7 collective-permute-start.26
  1195.5 2.7 collective-permute-start.29
  1195.6 6.9 collective-permute-start.28
  1202.7 7.2 collective-permute-start.31
  1204.1 5.8 collective-permute-start.30
  1560.5 2.7 collective-permute-start.33
  1560.6 6.9 collective-permute-start.32
  1567.7 6.9 collective-permute-start.35
  1569.1 5.5 collective-permute-start.34
  1575.2 5.1 collective-permute-start.37
  1575.3 6.9 collective-permute-start.36
  1582.3 8.8 collective-permute-start.39
  1585.7 5.4 collective-permute-start.38
  1591.8 2.7 collective-permute-start.41
  1592.1 6.8 collective-permute-start.40
  1599.1 9.5 collective-permute-start.43
  1602.9 5.7 collective-permute-start.42
  1609.1 2.7 collective-permute-start.45
  1609.2 6.9 collective-permute-start.44
  1616.3 6.5 collective-permute-start.47
  1618.5 4.2 collective-permute-start.46
  1623.5 2.7 collective-permute-start.49
  1623.6 6.9 collective-permute-start.48
  1630.6 8.5 collective-permute-start.51
  1633.6 5.5 collective-permute-start.50
  1639.7 2.9 collective-permute-start.53
  1640.0 6.9 collective-permute-start.52
  1647.1 6.6 collective-permute-start.55
  1649.4 4.2 collective-permute-start.54
  1654.5 6.9 collective-permute-start.56
  1661.5 8.5 collective-permute-start.59
  1664.5 5.5 collective-permute-start.58
  1670.6 2.7 collective-permute-start.61
  1670.7 6.9 collective-permute-start.60
  1677.8 6.6 collective-permute-start.63
  1680.1 4.2 collective-permute-start.62
  (23 other events, 1222.5 us)
